TPU v7x, 512 devices: a whole 4x4x16 slice. The times are simulated.
512 devices in a mesh: param: 32 (over y_lo, z), row: 4 (over x), col: 4 (over y_hi, core).
Axes of the slice: x: 4, y: 4 (y_hi: 2, y_lo: 2; y = y_hi * 2 + y_lo), z: 16, core: 2. Of those that a mesh axis runs over, the one named last changes fastest.
Arguments:
- coefficients: bfloat16 [3, 2, 32, 512], P(None, None, 'row', 'col'), may hold values from -6 to 6
- noise_sigma: float32 [2, 32, 512], P(None, 'row', 'col'), may hold values from 0.5 to 4
- residual: float32 [2, 32, 512], P(None, 'row', 'col'), may hold values from -0.6 to 0.6
- crack_mask: int32 [32, 4], P('row', 'col'), may hold values 0 or 1
- node_panel: bfloat16 [4, 64, 3, 2048], P('row', 'col', None, 'param'), may hold values from -0.41992188 to 0.41992188
Outputs:
- hessian: float32 [2048, 2048], P('param', ('row', 'col'))
- gradient: float32 [2048], P(('param', 'row', 'col'))
All inputs are finite; a program needn't handle non-finite values. No bound on the sum of `crack_mask` on one device may be relied on, other than what follows from the above.
Results may differ from a plain program's by a relative error of at most 0.0055.
Values may be sent and summed in bfloat16 or wider, within the bound.
No kernel may reach another device: no remote copies, remote signals or barrier semaphores. Data moves between devices by JAX's collectives and lax.ppermute only.
A program may use at most 64 MiB of HBM per device.

v0:
```python
import jax
import jax.numpy as jnp
from jax import lax
from jax.sharding import PartitionSpec as P

EL = 8
CAMS = 2


def shifted(block, axis, distance):
    devices = range(lax.axis_size(axis))
    route = [(i - distance, i) for i in devices if i - distance in devices]
    return lax.ppermute(block, axis, route)


def corner_shapes(rows, cols):
    vertical = ((jnp.arange(rows) % EL).astype(jnp.float32) + 0.5) / EL
    horizontal = ((jnp.arange(cols) % EL).astype(jnp.float32) + 0.5) / EL
    lower = vertical[:, None]
    right = horizontal[None, :]
    return jnp.stack(
        [(1.0 - lower) * (1.0 - right), (1.0 - lower) * right, lower * (1.0 - right), lower * right]
    )


def pixel_rows(design, extended):
    corners = jnp.stack(
        [extended[:-1, :-1], extended[:-1, 1:], extended[1:, :-1], extended[1:, 1:]], axis=2
    )
    width = extended.shape[3]
    corners = corners.reshape(design.shape[1], 12, width)
    sensitivity = jnp.einsum("kep,ekq->epq", design, corners, preferred_element_type=jnp.float32)
    return sensitivity.astype(jnp.bfloat16).reshape(design.shape[1] * design.shape[2], width)


def block_product(own_rows, other_rows):
    return lax.dot_general(
        own_rows, other_rows, (((0,), (0,)), ((), ())), preferred_element_type=jnp.float32
    )


def on_device(coefficients, noise_sigma, residual, crack_mask, node_panel):
    rows = noise_sigma.shape[1]
    cols = noise_sigma.shape[2]
    elem_rows = rows // EL
    elem_cols = cols // EL
    shapes = corner_shapes(rows, cols)
    live_rows = jnp.repeat(crack_mask.astype(jnp.float32), 128, axis=1)
    pixel_scale = live_rows[None] / noise_sigma
    design = (
        shapes[:, None, None] * pixel_scale[None, None] * coefficients.astype(jnp.float32)[None]
    ).astype(jnp.bfloat16)
    design = design.reshape(4, 3, CAMS, elem_rows, EL, elem_cols, EL).transpose(0, 1, 3, 5, 2, 4, 6)
    design = design.reshape(12, elem_rows * elem_cols, CAMS * EL * EL)
    weighted = (pixel_scale * residual).astype(jnp.bfloat16)
    weighted = (
        weighted.reshape(CAMS, elem_rows, EL, elem_cols, EL).transpose(1, 3, 0, 2, 4).reshape(-1)
    )
    right_edge = shifted(node_panel[:, :1], "col", -1)
    widened = jnp.concatenate([node_panel, right_edge], axis=1)
    lower_edge = shifted(widened, "row", -1)
    extended = jnp.concatenate([widened, lower_edge], axis=0)
    own_rows = pixel_rows(design, extended)
    grad_part = jnp.dot(weighted, own_rows, preferred_element_type=jnp.float32)
    block = block_product(
        own_rows, pixel_rows(design, lax.all_gather(extended, "param", axis=3, tiled=True))
    )
    hessian, gradient = (
        lax.psum_scatter(block, ("row", "col"), scatter_dimension=1, tiled=True),
        lax.psum_scatter(grad_part, ("row", "col"), scatter_dimension=0, tiled=True),
    )
    return (hessian, gradient)


def solution(mesh):
    in_specs = (
        P(None, None, "row", "col"),
        P(None, "row", "col"),
        P(None, "row", "col"),
        P("row", "col"),
        P("row", "col", None, "param"),
    )
    out_specs = (P("param", ("row", "col")), P(("param", "row", "col")))
    return jax.shard_map(
        on_device, mesh=mesh, in_specs=in_specs, out_specs=out_specs, check_vma=False
    )
```

profile of v0, /device:TPU:2, one launch (start us, length us, event | category | flops | bytes accessed | tf_op | source)
XLA Modules:
  0.0 247.3 jit_solution(17997718687711013562)
XLA Ops:
  7.2 0.7 slice.24
  7.9 1.3 collective-permute-start
  9.2 0.7 convert_bitcast_fusion
  9.9 0.8 multiply_convert_fusion.1
  10.7 0.1 mul.140
  10.9 0.9 reshape.255
  11.8 0.1 copy.29
  12.2 0.7 constant_dynamic-update-slice_fusion.1
  12.9 0.8 copy.30
  13.8 7.8 %collective-permute-start.1 = (bf16[1,17,3,64]{3,1,2,0:T(8,128)(2,1)S(1)}, bf16[1,17,3,64]{3,1,2,0:T(8,128)(2,1)S(1)}, u32[]{:S(2)}, u32[]{:S(2)}) collective-permute-start(bf16[1,17,3,64]{3,1,2,0:T(8,128)(2,1)S(1)} %constant_dynamic-update-slice_fusion), channel_id=1, source_target_pairs={{4,0},{8,4},{12,8},{5,1},{9,5},{13,9},{6,2},{10,6},{14,10},{7,3},{... | collective-permute-start | bytes 19592 | tf_op jit(solution)/shard_map/ppermute | solution.py:13
  21.5 0.6 slice_bitcast_fusion.2
  22.2 0.8 collective-permute-done.1
  23.0 0.6 copy-done
  23.6 0.1 copy.32
  23.8 85.1 %all_gather.3 = bf16[2,17,3,2048]{1,0,2,3:T(2,128)(2,1)S(1)} all-gather(bf16[2,17,3,64]{1,0,2,3:T(2,128)(2,1)S(1)} %copy.32), channel_id=1, replica_groups=mesh['param'=32,'row'=4,'col'=4] {'param'}, dimensions={3}, use_global_device_ids=true | all-gather | bytes 430848 | tf_op jit(solution)/shard_map/all_gather | solution.py:66
  108.9 13.9 %fusion.21 = (bf16[1,16,3,2048]{1,0,2,3:T(2,128)(2,1)}, bf16[1,16,3,2048]{1,0,2,3:T(2,128)(2,1)}, bf16[1,16,3,2048]{1,0,2,3:T(2,128)(2,1)}, bf16[1,16,3,2048]{1,0,2,3:T(2,128)(2,1)S(1)}) fusion(bf16[2,17,3,2048]{1,0,2,3:T(2,128)(2,1)S(1)} %all_gather.3), kind=kLoop, calls=%fused_computation.42 | loop fusion | bytes 1572864 | tf_op jit(solution)/shard_map/slice | solution.py:28
  122.8 6.5 %copy.41 = bf16[1,16,3,2048]{3,1,2,0:T(8,128)(2,1)S(1)} copy(bf16[1,16,3,2048]{1,0,2,3:T(2,128)(2,1)} %get-tuple-element.4) | data formatting | bytes 393216
  129.2 6.5 %copy.43 = bf16[1,16,3,2048]{3,1,2,0:T(8,128)(2,1)S(1)} copy(bf16[1,16,3,2048]{1,0,2,3:T(2,128)(2,1)} %get-tuple-element.5) | data formatting | bytes 393216
  135.7 7.8 %copy.42 = bf16[1,16,3,2048]{3,1,2,0:T(8,128)(2,1)} copy(bf16[1,16,3,2048]{1,0,2,3:T(2,128)(2,1)} %get-tuple-element.6) | data formatting | bytes 393216
  143.5 5.6 %copy.44 = bf16[1,16,3,2048]{3,1,2,0:T(8,128)(2,1)} copy(bf16[1,16,3,2048]{1,0,2,3:T(2,128)(2,1)S(1)} %get-tuple-element.7) | data formatting | bytes 393216
  149.1 0.8 slice_bitcast_fusion.1
  149.9 0.7 pad_maximum_fusion.2
  150.6 1.1 convolution_convert_fusion
  151.7 1.1 pad_maximum_fusion
  152.9 5.4 %fusion.4 = f32[64,2048]{1,0:T(8,128)} fusion(bf16[16,128,64]{1,2,0:T(8,128)(2,1)S(1)} %convolution_convert_fusion, bf16[12,16,128]{2,0,1:T(8,128)(2,1)} %copy.30, bf16[16,12,2048]{2,0,1:T(8,128)(2,1)S(1)} %bitcast.44), kind=kOutput, calls=%fused_computation.3 | convolution fusion | flops 641728512 | bytes 1622016 | tf_op jit(solution)/shard_map/dot_general | solution.py:37
  158.3 0.1 reshape.252
  158.5 0.1 reshape.257
  158.6 1.3 dynamic-slice
  160.5 0.2 convolution_bitcast_fusion
  160.7 29.3 %all-reduce = f32[64]{0:T(128)S(1)} all-reduce(f32[64]{0:T(128)S(1)} %convolution_bitcast_fusion), channel_id=3, replica_groups=mesh['param'=32,'row'=4,'col'=4] {'row','col'}, use_global_device_ids=true, to_apply=%region_1.2.clone | all-reduce | flops 64 | bytes 512
  190.0 0.6 dynamic-slice.1
  190.6 49.9 %reduce-scatter.2.cloned.1.call-done = f32[64,128]{1,0:T(8,128)} async-done(((f32[64,2048]{1,0:T(8,128)}), f32[64,128]{1,0:T(8,128)}) %reduce-scatter.2.cloned.1.call-update) | async-done | bytes 32784 | tf_op jit(solution)/shard_map/reduce_scatter | solution.py:69
  (16 shorter events, 0.4 us)
Async XLA Ops:
  7.2 233.3 %reduce-scatter.2.cloned.1.call-start = ((), (), s32[]{:S(2)}) async-start(), calls=%async_computation.1 | async-start | bytes 557056 | tf_op jit(solution)/shard_map/reduce_scatter | solution.py:69
  7.9 5.8 %collective-permute-start = (bf16[1,1,3,64]{3,1,2,0:T(2,128)(2,1)S(1)}, bf16[1,1,3,64]{3,1,2,0:T(2,128)(2,1)S(1)}, u32[]{:S(2)}, u32[]{:S(2)}) collective-permute-start(bf16[1,1,3,64]{3,1,2,0:T(2,128)(2,1)S(1)} %slice.24), channel_id=1, source_target_pairs={{1,0},{2,1},{3,2},{5,4},{6,5},{7,6},{9,8},{10,9},{11,10},{13,12},{... | collective-permute-start | bytes 1160 | tf_op jit(solution)/shard_map/ppermute | solution.py:13
  13.8 9.2 %collective-permute-start.1 = (bf16[1,17,3,64]{3,1,2,0:T(8,128)(2,1)S(1)}, bf16[1,17,3,64]{3,1,2,0:T(8,128)(2,1)S(1)}, u32[]{:S(2)}, u32[]{:S(2)}) collective-permute-start(bf16[1,17,3,64]{3,1,2,0:T(8,128)(2,1)S(1)} %constant_dynamic-update-slice_fusion), channel_id=1, source_target_pairs={{4,0},{8,4},{12,8},{5,1},{9,5},{13,9},{6,2},{10,6},{14,10},{7,3},{... | collective-permute-start | bytes 19592 | tf_op jit(solution)/shard_map/ppermute | solution.py:13
  23.0 0.6 copy-start
  135.7 14.2 %copy-start.1 = (bf16[1,16,3,64]{3,1,2,0:T(8,128)(2,1)S(1)}, bf16[1,16,3,64]{3,1,2,0:T(8,128)(2,1)}, u32[]{:S(2)}) copy-start(bf16[1,16,3,64]{3,1,2,0:T(8,128)(2,1)} %param.9) | copy-start | bytes 18436
Sparse Core Ops, SparseCore 0:
  158.4 81.9 reduce-scatter.1
where the time goes:
time: 248 us; the launch traced here: 247 us
  blocking collectives  114 us (46%)
  waiting for transfers between devices  50.7 us (20%)
  local copies, waits for them, and re-layouts  48 us (19%)
  between operations  14.8 us (6%)
  starting transfers between devices  9.1 us (4%)
  matrix products  6.69 us (3%)
  other arithmetic  3.54 us (1%)
    all_gather x1, blocking collectives, on_device(): lax.all_gather(extended, 'param', axis=3, tiled=True)  85.1 us
    reduce_scatter x1, waiting for transfers between devices, on_device(): lax.psum_scatter(block, ('row', 'col'), scatter_dimension=1, tiled=True)  49.9 us
    unnamed x11, local copies, waits for them, and re-layouts  29.5 us
    unnamed x1, blocking collectives  29.3 us
    slice x1, local copies, waits for them, and re-layouts, pixel_rows(): extended[:-1, :-1]  13.9 us
    ppermute x2, starting transfers between devices, shifted(): return lax.ppermute(block, axis, route)  9.07 us
    dot_general x1, matrix products, block_product(): lax.dot_general(own_rows, other_rows, (((0,), (0,)), ((), ())), preferred...  5.42 us
  transfers between devices with their start and end apart: 3, of which 2 were waited for; matrix products, arithmetic and copies ran while one was open for 3% of the time, Pallas kernels for 0%

commit v1 on v0

--- a/solution.py
+++ b/solution.py
@@ -63,7 +63,14 @@
     own_rows = pixel_rows(design, extended)
     grad_part = jnp.dot(weighted, own_rows, preferred_element_type=jnp.float32)
     block = block_product(
-        own_rows, pixel_rows(design, lax.all_gather(extended, "param", axis=3, tiled=True))
+        own_rows,
+        pixel_rows(
+            design,
+            jnp.concatenate(
+                lax.all_to_all(jnp.stack([extended] * lax.axis_size("param")), "param", 0, 0),
+                axis=3,
+            ),
+        ),
     )
     hessian, gradient = (
         lax.psum_scatter(block, ("row", "col"), scatter_dimension=1, tiled=True),

time: 248 us -> 161 us (0.65)
  blocking collectives: 114 us -> 28.6 us
  local copies, waits for them, and re-layouts: 48 us -> 10.8 us
  waiting for transfers between devices: 50.7 us -> 77.2 us
  starting transfers between devices: 9.1 us -> 22 us
    all_gather x1 -> x0, blocking collectives: 85.1 us -> none  [on_device(): lax.all_gather(extended, 'param', axis=3, tiled=True)]
    all_to_all x0 -> x1, waiting for transfers between devices: none -> 26.9 us  [on_device(): lax.all_to_all(jnp.stack([extended] * lax.axis_size('param')), 'param', 0...]
    unnamed x11 -> x8, local copies, waits for them, and re-layouts: 29.5 us -> 5.44 us
    slice x1, local copies, waits for them, and re-layouts: 13.9 us -> 0.97 us  [pixel_rows(): extended[:-1, :-1]]
    all_to_all x0 -> x1, starting transfers between devices: none -> 12.9 us  [on_device(): lax.all_to_all(jnp.stack([extended] * lax.axis_size('param')), 'param', 0...]
  transfers between devices with their start and end apart: 3 -> 4, of which waited for: 2 -> 3; matrix products, arithmetic and copies ran while one was open for 3% -> 4% of each run, Pallas kernels for 0% -> 0%
where the time goes in v1:
time: 161 us; the launch traced here: 160 us
  waiting for transfers between devices  77.2 us (48%)
  blocking collectives  28.6 us (18%)
  starting transfers between devices  22 us (14%)
  between operations  14.9 us (9%)
  local copies, waits for them, and re-layouts  10.8 us (7%)
  matrix products  5.02 us (3%)
  other arithmetic  1.79 us (1%)
    reduce_scatter x1, waiting for transfers between devices, on_device(): lax.psum_scatter(block, ('row', 'col'), scatter_dimension=1, tiled=True)  50.1 us
    unnamed x1, blocking collectives  28.6 us
    all_to_all x1, waiting for transfers between devices, on_device(): lax.all_to_all(jnp.stack([extended] * lax.axis_size('param')), 'param', 0...  26.9 us
    all_to_all x1, starting transfers between devices, on_device(): lax.all_to_all(jnp.stack([extended] * lax.axis_size('param')), 'param', 0...  12.9 us
    ppermute x2, starting transfers between devices, shifted(): return lax.ppermute(block, axis, route)  9.07 us
    unnamed x8, local copies, waits for them, and re-layouts  5.44 us
    dot_general x1, matrix products, block_product(): lax.dot_general(own_rows, other_rows, (((0,), (0,)), ((), ())), preferred...  4.58 us
  transfers between devices with their start and end apart: 4, of which 3 were waited for; matrix products, arithmetic and copies ran while one was open for 4% of the time, Pallas kernels for 0%

profile of v1, /device:TPU:2, one launch (start us, length us, event | category | flops | bytes accessed | tf_op | source)
XLA Modules:
  0.0 160.3 jit_solution(477045634303549122)
XLA Ops:
  7.2 0.7 slice.24
  7.9 1.3 collective-permute-start
  9.1 0.7 constant_dynamic-update-slice_fusion.1
  9.9 0.7 convert_bitcast_fusion
  10.5 0.8 multiply_convert_fusion.1
  11.3 7.8 %collective-permute-start.1 = (bf16[1,17,3,64]{3,1,2,0:T(8,128)(2,1)S(1)}, bf16[1,17,3,64]{3,1,2,0:T(8,128)(2,1)S(1)}, u32[]{:S(2)}, u32[]{:S(2)}) collective-permute-start(bf16[1,17,3,64]{3,1,2,0:T(8,128)(2,1)S(1)} %constant_dynamic-update-slice_fusion), channel_id=1, source_target_pairs={{4,0},{8,4},{12,8},{5,1},{9,5},{13,9},{6,2},{10,6},{14,10},{7,3},{... | collective-permute-start | bytes 19592 | tf_op jit(solution)/shard_map/ppermute | solution.py:13
  19.3 0.9 reshape.265
  20.3 0.1 copy.81
  20.4 0.1 collective-permute-done.1
  20.6 0.4 broadcast_bitcast_fusion
  21.1 1.3 reshape.271
  22.4 12.9 %all-to-all-start = ((bf16[32,2,3264]{2,1,0:T(2,128)(2,1)}), bf16[32,2,3264]{2,1,0:T(2,128)(2,1)S(1)}, u32[]{:S(2)}, u32[]{:S(2)}) async-start(bf16[32,2,3264]{2,1,0:T(2,128)(2,1)} %reshape.271), calls=%async_computation | async-start | bytes 851968 | tf_op jit(solution)/shard_map/all_to_all | solution.py:70
  35.6 0.2 copy.82
  35.9 0.3 copy-done
  36.2 0.3 convolution_convert_fusion
  36.5 26.9 %all-to-all-done = bf16[32,2,3264]{2,1,0:T(2,128)(2,1)S(1)} async-done(((bf16[32,2,3264]{2,1,0:T(2,128)(2,1)}), bf16[32,2,3264]{2,1,0:T(2,128)(2,1)S(1)}, u32[]{:S(2)}, u32[]{:S(2)}) %all-to-all-start) | async-done | bytes 417824 | tf_op jit(solution)/shard_map/all_to_all | solution.py:70
  63.4 0.8 reshape.272
  64.2 0.6 bitcast_bitcast_fusion
  64.8 0.2 copy.85
  65.0 0.6 reshape.260
  65.6 1.0 fusion.21
  66.6 0.2 copy_bitcast_fusion.2
  66.8 0.2 copy_bitcast_fusion
  67.0 0.1 pad_maximum_fusion
  67.2 4.6 %fusion.4 = f32[64,2048]{1,0:T(8,128)} fusion(bf16[16,128,64]{1,2,0:T(8,128)(2,1)S(1)} %convolution_convert_fusion, bf16[12,16,128]{2,0,1:T(8,128)(2,1)S(1)} %copy.82, bf16[16,12,2048]{2,0,1:T(8,128)(2,1)S(1)} %bitcast.54), kind=kOutput, calls=%fused_computation.3 | convolution fusion | flops 641728512 | bytes 1622016 | tf_op jit(solution)/shard_map/dot_general | solution.py:37
  71.8 0.1 reshape.262
  71.9 0.1 reshape.267
  72.0 1.3 dynamic-slice
  74.0 0.2 convolution_bitcast_fusion
  74.1 28.6 %all-reduce = f32[64]{0:T(128)S(1)} all-reduce(f32[64]{0:T(128)S(1)} %convolution_bitcast_fusion), channel_id=3, replica_groups=mesh['param'=32,'row'=4,'col'=4] {'row','col'}, use_global_device_ids=true, to_apply=%region_1.2.clone | all-reduce | flops 64 | bytes 512
  102.8 0.6 dynamic-slice.1
  103.3 50.1 %reduce-scatter.2.cloned.1.call-done = f32[64,128]{1,0:T(8,128)} async-done(((f32[64,2048]{1,0:T(8,128)}), f32[64,128]{1,0:T(8,128)}) %reduce-scatter.2.cloned.1.call-update) | async-done | bytes 32784 | tf_op jit(solution)/shard_map/reduce_scatter | solution.py:76
  (19 shorter events, 0.6 us)
Async XLA Ops:
  7.9 3.5 %collective-permute-start = (bf16[1,1,3,64]{3,1,2,0:T(2,128)(2,1)S(1)}, bf16[1,1,3,64]{3,1,2,0:T(2,128)(2,1)S(1)}, u32[]{:S(2)}, u32[]{:S(2)}) collective-permute-start(bf16[1,1,3,64]{3,1,2,0:T(2,128)(2,1)S(1)} %slice.24), channel_id=1, source_target_pairs={{1,0},{2,1},{3,2},{5,4},{6,5},{7,6},{9,8},{10,9},{11,10},{13,12},{... | collective-permute-start | bytes 1160 | tf_op jit(solution)/shard_map/ppermute | solution.py:13
  11.3 9.2 %collective-permute-start.1 = (bf16[1,17,3,64]{3,1,2,0:T(8,128)(2,1)S(1)}, bf16[1,17,3,64]{3,1,2,0:T(8,128)(2,1)S(1)}, u32[]{:S(2)}, u32[]{:S(2)}) collective-permute-start(bf16[1,17,3,64]{3,1,2,0:T(8,128)(2,1)S(1)} %constant_dynamic-update-slice_fusion), channel_id=1, source_target_pairs={{4,0},{8,4},{12,8},{5,1},{9,5},{13,9},{6,2},{10,6},{14,10},{7,3},{... | collective-permute-start | bytes 19592 | tf_op jit(solution)/shard_map/ppermute | solution.py:13
  22.4 41.0 %all-to-all-start = ((bf16[32,2,3264]{2,1,0:T(2,128)(2,1)}), bf16[32,2,3264]{2,1,0:T(2,128)(2,1)S(1)}, u32[]{:S(2)}, u32[]{:S(2)}) async-start(bf16[32,2,3264]{2,1,0:T(2,128)(2,1)} %reshape.271), calls=%async_computation | async-start | bytes 851968 | tf_op jit(solution)/shard_map/all_to_all | solution.py:70
  35.3 118.2 %reduce-scatter.2.cloned.1.call-start = ((), (), s32[]{:S(2)}) async-start(), calls=%async_computation.2 | async-start | bytes 557056 | tf_op jit(solution)/shard_map/reduce_scatter | solution.py:76
  35.5 0.7 copy-start
Sparse Core Ops, SparseCore 0:
  71.9 81.5 reduce-scatter.1
